TPU v7x, 256 devices: a whole 4x4x8 slice. The times are simulated.
256 devices in a mesh: row: 2 (over core), col: 2 (over x_lo), rhs: 64 (over z, y, x_hi).
Axes of the slice: x: 4 (x_hi: 2, x_lo: 2; x = x_hi * 2 + x_lo), y: 4, z: 8, core: 2. Of those that a mesh axis runs over, the one named last changes fastest.
Arguments:
- front: bfloat16 [4096, 4096], P(('row', 'rhs'), 'col'), as said below
- anc_weight: bfloat16 [1024, 4096], P(('row', 'rhs'), 'col'), may hold values from -0.1875 to 0.1875
- solved: bfloat16 [2048, 8192], P(('row', 'col'), 'rhs'), may hold values from -6 to 6
- owners: int32 [8], replicated, may hold values from 0 to 3, as said below
- indices: int32 [8, 128], replicated, may hold values from 0 to 511
- counts: int32 [8], replicated, may hold values from 64 to 128, as said below
- rhs_side: bfloat16 [4096, 8192], P('row', 'rhs'), may hold values from -6 to 6
Outputs:
- solution: bfloat16 [4096, 8192], P('row', 'rhs')
Inputs may be any that keep to these rules, and one draw needn't show every extreme that they name: `front`: zero above the diagonal; diagonal entries 1 or more. The 4 tiles of each aligned block of 4 tiles have 4 different owners, numbered row index times 2 plus col index. `counts`: rows at or past a tile's count are padding.
All inputs are finite; a program needn't handle non-finite values.
Results may differ from a plain program's by a relative error of at most 0.0038.
Values may be sent and summed in bfloat16 or wider, within the bound.
No kernel may reach another device: no remote copies, remote signals or barrier semaphores. Data moves between devices by JAX's collectives and lax.ppermute only.
A program may use at most 128 MiB of HBM per device.

v0:
```python
import jax
import jax.numpy as jnp
from jax import lax
from jax.sharding import PartitionSpec as P

BLOCK = 128
HIGH = lax.Precision.HIGHEST


def split_dot_t(mat_bf16, vec_f32):
    hi = vec_f32.astype(jnp.bfloat16)
    lo = (vec_f32 - hi.astype(jnp.float32)).astype(jnp.bfloat16)
    dims = (((0,), (0,)), ((), ()))
    out = lax.dot_general(mat_bf16, hi, dims, preferred_element_type=jnp.float32)
    return out + lax.dot_general(mat_bf16, lo, dims, preferred_element_type=jnp.float32)


def prepare(tile):
    n = tile.shape[0]
    nb = n // BLOCK
    blocks = jnp.stack(
        [tile[j * BLOCK : (j + 1) * BLOCK, j * BLOCK : (j + 1) * BLOCK] for j in range(nb)]
    ).astype(jnp.float32)
    eye = jnp.eye(BLOCK, dtype=jnp.float32)
    diag = jnp.sum(blocks * eye[None], axis=2)
    lower = jnp.tril(jnp.ones((BLOCK, BLOCK), jnp.bool_), -1)
    nil = jnp.where(lower[None], blocks / diag[:, :, None], 0.0)
    prod = eye[None] - nil
    power = nil
    steps = 1
    while 2**steps < BLOCK:
        power = jnp.einsum("bij,bjk->bik", power, power, precision=HIGH)
        prod = jnp.einsum("bij,bjk->bik", prod, eye[None] + power, precision=HIGH)
        steps += 1
    return (prod, 1.0 / diag)


def apply_solve(tile, prod, inv_diag, rhs):
    n = tile.shape[0]
    nb = n // BLOCK
    cols = rhs.shape[1]

    def body(i, carry):
        rest, out = carry
        j = nb - 1 - i
        r_j = lax.dynamic_slice_in_dim(rest, j * BLOCK, BLOCK, 0)
        p_j = lax.dynamic_index_in_dim(prod, j, 0, keepdims=False)
        d_j = lax.dynamic_index_in_dim(inv_diag, j, 0, keepdims=False)
        v_j = jnp.einsum("ji,jk->ik", p_j, r_j, precision=HIGH) * d_j[:, None]
        rows = lax.dynamic_slice_in_dim(tile, j * BLOCK, BLOCK, 0)
        rest = rest - split_dot_t(rows, v_j)
        out = lax.dynamic_update_slice_in_dim(out, v_j, j * BLOCK, 0)
        return (rest, out)

    _, out = lax.fori_loop(0, nb, body, (rhs, jnp.zeros((n, cols), jnp.float32)))
    return out


def on_device(front, anc_weight, solved, owners, indices, counts, rhs_side):
    row_count = lax.axis_size("row")
    col_count = lax.axis_size("col")
    tiles_block = row_count * col_count
    row_index = lax.axis_index("row")
    col_index = lax.axis_index("col")
    tile_rows = indices.shape[1]
    columns = solved.shape[1]
    self_id = row_index * col_count + col_index
    owner_grid = owners.reshape(row_count, tiles_block)
    mine = (owner_grid == self_id).astype(jnp.int32)
    position = jnp.sum(mine * jnp.arange(tiles_block, dtype=jnp.int32)[None, :], axis=1)
    tile_ids = jnp.arange(row_count, dtype=jnp.int32) * tiles_block + position
    local_rows = indices[tile_ids]
    live_rows = jnp.arange(tile_rows, dtype=jnp.int32)[None, :] < counts[tile_ids][:, None]
    picked = solved[local_rows.reshape(-1)].reshape(row_count, tile_rows, columns)
    picked = jnp.where(live_rows[:, :, None], picked, jnp.zeros_like(picked))
    block_owners = lax.dynamic_slice_in_dim(owners, row_index * tiles_block, tiles_block)
    outgoing = jnp.broadcast_to(picked[:, None], (row_count, col_count, tile_rows, columns))
    outgoing = outgoing.reshape(row_count * col_count * tile_rows, columns)
    received = lax.all_to_all(outgoing, ("row", "col"), split_axis=0, concat_axis=0, tiled=True)
    slot_rows = received.reshape(tiles_block, tile_rows, columns)
    anc_values = slot_rows[block_owners].reshape(tiles_block * tile_rows, columns)
    weight_tile = lax.all_gather(anc_weight, "rhs", axis=0, tiled=True)
    front_tile = lax.all_gather(front, "rhs", axis=0, tiled=True)
    width = front_tile.shape[1]
    anc_total = lax.dot_general(
        weight_tile, anc_values, (((0,), (0,)), ((), ())), preferred_element_type=jnp.float32
    )
    prod, inv_diag = prepare(front_tile)
    rhs_values = rhs_side.astype(jnp.float32)
    down = [(1, 0)]
    left = [(1, 0)]
    right = [(0, 1)]
    own_one = anc_total.astype(jnp.bfloat16)
    other_one = lax.ppermute(own_one, "row", [(0, 1)])
    reduced_one = rhs_values - own_one.astype(jnp.float32) - other_one.astype(jnp.float32)
    sol_one = apply_solve(front_tile, prod, inv_diag, reduced_one).astype(jnp.bfloat16)
    got_one = lax.ppermute(sol_one, "col", left)
    sol_one = jnp.where(col_index == 1, sol_one, got_one)
    own_zero = (anc_total + split_dot_t(front_tile, sol_one.astype(jnp.float32))).astype(
        jnp.bfloat16
    )
    own_zero = jnp.where(row_index == 0, anc_total.astype(jnp.bfloat16), own_zero)
    other_zero = lax.ppermute(own_zero, "row", down)
    reduced_zero = rhs_values - own_zero.astype(jnp.float32) - other_zero.astype(jnp.float32)
    sol_zero = apply_solve(front_tile, prod, inv_diag, reduced_zero).astype(jnp.bfloat16)
    got_zero = lax.ppermute(sol_zero, "col", right)
    sol_zero = jnp.where(col_index == 0, sol_zero, got_zero)
    return jnp.where(row_index == 1, sol_one, sol_zero)


def solution(mesh):
    placed = (
        P(("row", "rhs"), "col"),
        P(("row", "rhs"), "col"),
        P(("row", "col"), "rhs"),
        P(),
        P(),
        P(),
        P("row", "rhs"),
    )
    return jax.shard_map(
        on_device, mesh=mesh, in_specs=placed, out_specs=P("row", "rhs"), check_vma=False
    )
```

profile of v0, /device:TPU:2, one launch (start us, length us, event | category | flops | bytes accessed | tf_op | source)
XLA Modules:
  0.0 487.1 jit_solution(5792975368108984710)
XLA Ops:
  13.2 5.5 %all-to-all-start = ((bf16[4,128,128]{2,1,0:T(8,128)(2,1)}), bf16[4,128,128]{2,1,0:T(8,128)(2,1)S(1)}, u32[]{:S(2)}, u32[]{:S(2)}) async-start(bf16[4,128,128]{2,1,0:T(8,128)(2,1)} %bitcast.9), calls=%async_computation | async-start | bytes 262144 | tf_op jit(solution)/shard_map/all_to_all | solution.py:79
  19.5 2.0 all-to-all-done
  22.1 109.4 %all-gather.3.cloned.1.call-done = bf16[512,2048]{1,0:T(8,128)(2,1)} async-done(((bf16[8,2048]{1,0:T(8,128)(2,1)}), bf16[512,2048]{1,0:T(8,128)(2,1)}) %all-gather.3.cloned.1.call-update) | async-done | bytes 2097168 | tf_op jit(solution)/shard_map/all_gather | solution.py:82
  131.5 2.1 fusion.80
  137.7 1.5 copy.12
  139.2 142.6 %all-gather.5.cloned.1.call-done = bf16[2048,2048]{1,0:T(8,128)(2,1)} async-done(((bf16[32,2048]{1,0:T(8,128)(2,1)}), bf16[2048,2048]{1,0:T(8,128)(2,1)}) %all-gather.5.cloned.1.call-update) | async-done | bytes 8388624 | tf_op jit(solution)/shard_map/all_gather | solution.py:83
  294.5 1.5 fusion.45
  308.1 2.2 fusion.85
  310.4 64.9 %while.34 = (s32[]{:T(128)}, f32[2048,128]{1,0:T(8,128)S(1)}, bf16[2048,128]{1,0:T(8,128)(2,1)S(1)}, bf16[2048,2048]{1,0:T(8,128)(2,1)}, f32[16,128,128]{2,1,0:T...) while((s32[]{:T(128)}, f32[2048,128]{1,0:T(8,128)S(1)}, ...), condition=%wide.region_3.4_spmd, body=%wide.region_2.3_spmd.sunk | while | flops 160006144 | bytes 5639389 | solution.py:55
  313.0 1.5 fusion.124
  317.0 1.5 fusion.124
  321.1 1.5 fusion.124
  325.1 1.5 fusion.124
  333.2 1.5 fusion.124
  341.4 1.5 fusion.124
  349.5 1.5 fusion.124
  357.6 1.5 fusion.124
  365.7 1.5 fusion.124
  373.8 1.5 fusion.124
  375.3 3.4 collective-permute-start.1
  378.7 8.0 %collective-permute-done.1 = bf16[2048,128]{1,0:T(8,128)(2,1)S(1)} collective-permute-done((bf16[2048,128]{1,0:T(8,128)(2,1)S(1)}, bf16[2048,128]{1,0:T(8,128)(2,1)S(1)}, u32[]{:S(2)}, u32[]{:S(2)}) %collective-permute-start.1) | collective-permute-done | bytes 524320 | tf_op jit(solution)/shard_map/ppermute | solution.py:97
  386.8 4.8 fusion.48
  394.3 2.5 collective-permute-done.2
  398.4 64.9 %while.35 = (s32[]{:T(128)}, f32[2048,128]{1,0:T(8,128)S(1)}, bf16[2048,128]{1,0:T(8,128)(2,1)S(1)}, bf16[2048,2048]{1,0:T(8,128)(2,1)}, f32[16,128,128]{2,1,0:T...) while((s32[]{:T(128)}, f32[2048,128]{1,0:T(8,128)S(1)}, ...), condition=%wide.region_5.6_spmd, body=%wide.region_4.5_spmd.sunk | while | flops 160006144 | bytes 5639389 | solution.py:55
  405.1 1.5 fusion.130
  409.1 1.5 fusion.130
  413.2 1.5 fusion.130
  417.2 1.5 fusion.130
  425.4 1.5 fusion.130
  437.5 1.5 fusion.130
  449.7 1.5 fusion.130
  464.7 14.7 %collective-permute-done.3 = bf16[2048,128]{1,0:T(8,128)(2,1)S(1)} collective-permute-done((bf16[2048,128]{1,0:T(8,128)(2,1)S(1)}, bf16[2048,128]{1,0:T(8,128)(2,1)S(1)}, u32[]{:S(2)}, u32[]{:S(2)}) %collective-permute-start.3) | collective-permute-done | bytes 524320 | tf_op jit(solution)/shard_map/ppermute | solution.py:106
  (184 shorter events, 146.4 us)
Async XLA Ops:
  6.5 4.9 %copy-start = (bf16[512,128]{1,0:T(8,128)(2,1)S(1)}, bf16[512,128]{1,0:T(8,128)(2,1)}, u32[]{:S(2)}) copy-start(bf16[512,128]{1,0:T(8,128)(2,1)} %param.13) | copy-start | bytes 393220
  6.5 125.0 %all-gather.3.cloned.1.call-start = ((), (), s32[]{:S(2)}) async-start(), calls=%async_computation.1 | async-start | bytes 2129920 | tf_op jit(solution)/shard_map/all_gather | solution.py:82
  7.3 274.6 %all-gather.5.cloned.1.call-start = ((), (), s32[]{:S(2)}) async-start(), calls=%async_computation.2 | async-start | bytes 8519680 | tf_op jit(solution)/shard_map/all_gather | solution.py:83
  13.2 8.3 %all-to-all-start = ((bf16[4,128,128]{2,1,0:T(8,128)(2,1)}), bf16[4,128,128]{2,1,0:T(8,128)(2,1)S(1)}, u32[]{:S(2)}, u32[]{:S(2)}) async-start(bf16[4,128,128]{2,1,0:T(8,128)(2,1)} %bitcast.9), calls=%async_computation | async-start | bytes 262144 | tf_op jit(solution)/shard_map/all_to_all | solution.py:79
  133.6 2.8 collective-permute-start
  375.3 11.4 %collective-permute-start.1 = (bf16[2048,128]{1,0:T(8,128)(2,1)S(1)}, bf16[2048,128]{1,0:T(8,128)(2,1)S(1)}, u32[]{:S(2)}, u32[]{:S(2)}) collective-permute-start(bf16[2048,128]{1,0:T(8,128)(2,1)S(1)} %get-tuple-element.313), channel_id=1, source_target_pairs={{64,0},{65,1},{66,2},{67,3},{68,4},{69,5},{70,6},{71,7},{72,8},{73... | collective-permute-start | bytes 1572872 | tf_op jit(solution)/shard_map/ppermute | solution.py:97
  378.7 12.9 %slice-start = ((s8[8388608]{0:T(1024)(128)(4,1)}), s8[4194304]{0:T(1024)(128)(4,1)S(1)}, s32[]{:S(2)}) async-start(s8[8388608]{0:T(1024)(128)(4,1)} %bitcast.128), calls=%async_computation.3 | async-start | bytes 8388608
  386.8 4.8 slice-start.1
  393.0 1.3 copy-start.1
  393.0 3.8 collective-permute-start.2
  463.4 16.0 %collective-permute-start.3 = (bf16[2048,128]{1,0:T(8,128)(2,1)S(1)}, bf16[2048,128]{1,0:T(8,128)(2,1)S(1)}, u32[]{:S(2)}, u32[]{:S(2)}) collective-permute-start(bf16[2048,128]{1,0:T(8,128)(2,1)S(1)} %get-tuple-element.314), channel_id=1, source_target_pairs={{0,64},{1,65},{2,66},{3,67},{4,68},{5,69},{6,70},{7,71},{8,72},{9,... | collective-permute-start | bytes 1572872 | tf_op jit(solution)/shard_map/ppermute | solution.py:106
Sparse Core Ops, SparseCore 0:
  10.9 120.5 all-gather.2
  135.0 146.8 all-gather.4
where the time goes:
time: 493 us; the launch traced here: 487 us
  waiting for transfers between devices  281 us (57%)
  matrix products  152 us (31%)
  local copies, waits for them, and re-layouts  20.6 us (4%)
  between operations  13.7 us (3%)
  starting transfers between devices  12.9 us (3%)
  other arithmetic  5.61 us (1%)
    all_gather x1, waiting for transfers between devices, on_device(): front_tile = lax.all_gather(front, 'rhs', axis=0, tiled=True)  143 us
    all_gather x1, waiting for transfers between devices, on_device(): weight_tile = lax.all_gather(anc_weight, 'rhs', axis=0, tiled=True)  109 us
    dot_general x33, matrix products, split_dot_t(): lax.dot_general(mat_bf16, lo, dims, preferred_element_type=jnp.float32)  51.9 us
    dot_general x33, matrix products, split_dot_t(): lax.dot_general(mat_bf16, hi, dims, preferred_element_type=jnp.float32)  45.5 us
    dot_general x32, matrix products, body(): v_j = jnp.einsum('ji,jk->ik', p_j, r_j, precision=HIGH) * d_j[:, None]  36.7 us
    ppermute x1, waiting for transfers between devices, on_device(): got_zero = lax.ppermute(sol_zero, 'col', right)  14.7 us
    unnamed x24, local copies, waits for them, and re-layouts  12.7 us
  transfers between devices with their start and end apart: 7, of which 7 were waited for; matrix products, arithmetic and copies ran while one was open for 3% of the time, Pallas kernels for 0%

commit v1 on v0

--- a/solution.py
+++ b/solution.py
@@ -80,7 +80,15 @@
     slot_rows = received.reshape(tiles_block, tile_rows, columns)
     anc_values = slot_rows[block_owners].reshape(tiles_block * tile_rows, columns)
     weight_tile = lax.all_gather(anc_weight, "rhs", axis=0, tiled=True)
-    front_tile = lax.all_gather(front, "rhs", axis=0, tiled=True)
+    front_tile = jnp.concatenate(
+        lax.all_to_all(
+            jnp.stack([front for _ in range(lax.axis_size("rhs"))], axis=0),
+            "rhs",
+            split_axis=0,
+            concat_axis=0,
+        ),
+        axis=0,
+    )
     width = front_tile.shape[1]
     anc_total = lax.dot_general(
         weight_tile, anc_values, (((0,), (0,)), ((), ())), preferred_element_type=jnp.float32

time: 493 us -> 450 us (0.913)
  waiting for transfers between devices: 281 us -> 214 us
  starting transfers between devices: 12.9 us -> 20.7 us
  blocking collectives: 0 us -> 7.4 us
    all_gather x1 -> x0, waiting for transfers between devices: 143 us -> none  [on_device(): front_tile = lax.all_gather(front, 'rhs', axis=0, tiled=True)]
    all_gather x1, waiting for transfers between devices: 109 us -> 168 us  [on_device(): weight_tile = lax.all_gather(anc_weight, 'rhs', axis=0, tiled=True)]
    all_to_all x1, waiting for transfers between devices: 2.04 us -> 18.6 us  [on_device(): lax.all_to_all(jnp.stack([front for _ in range(lax.axis_size('rhs'))], ax...]
    all_to_all x0 -> x1, blocking collectives: none -> 7.4 us  [on_device(): lax.all_to_all(outgoing, ('row', 'col'), split_axis=0, concat_axis=0, til...]
    all_to_all x1, starting transfers between devices: 5.53 us -> 12.6 us  [on_device(): lax.all_to_all(jnp.stack([front for _ in range(lax.axis_size('rhs'))], ax...]
    another operation x2 -> x3, local copies, waits for them, and re-layouts: 0.14 us -> 5.34 us  [the longest x1 5.2 us: on_device(): jnp.stack([front for _ in range(lax.axis_size('rhs'))], axis=0)]
  transfers between devices with their start and end apart: 7 -> 6, of which waited for: 7 -> 6; matrix products, arithmetic and copies ran while one was open for 3% -> 1% of each run, Pallas kernels for 0% -> 0%
where the time goes in v1:
time: 450 us; the launch traced here: 442 us
  waiting for transfers between devices  214 us (48%)
  matrix products  155 us (34%)
  local copies, waits for them, and re-layouts  24.1 us (5%)
  starting transfers between devices  20.7 us (5%)
  between operations  13.7 us (3%)
  blocking collectives  7.4 us (2%)
  other arithmetic  4.92 us (1%)
    all_gather x1, waiting for transfers between devices, on_device(): weight_tile = lax.all_gather(anc_weight, 'rhs', axis=0, tiled=True)  168 us
    dot_general x33, matrix products, split_dot_t(): lax.dot_general(mat_bf16, lo, dims, preferred_element_type=jnp.float32)  51.7 us
    dot_general x33, matrix products, split_dot_t(): lax.dot_general(mat_bf16, hi, dims, preferred_element_type=jnp.float32)  48.9 us
    dot_general x32, matrix products, body(): v_j = jnp.einsum('ji,jk->ik', p_j, r_j, precision=HIGH) * d_j[:, None]  36.7 us
    all_to_all x1, waiting for transfers between devices, on_device(): lax.all_to_all(jnp.stack([front for _ in range(lax.axis_size('rhs'))], ax...  18.6 us
    ppermute x1, waiting for transfers between devices, on_device(): got_zero = lax.ppermute(sol_zero, 'col', right)  14.7 us
    all_to_all x1, starting transfers between devices, on_device(): lax.all_to_all(jnp.stack([front for _ in range(lax.axis_size('rhs'))], ax...  12.6 us
    unnamed x24, local copies, waits for them, and re-layouts  11.7 us
  transfers between devices with their start and end apart: 6, of which 6 were waited for; matrix products, arithmetic and copies ran while one was open for 1% of the time, Pallas kernels for 0%

profile of v1, /device:TPU:2, one launch (start us, length us, event | category | flops | bytes accessed | tf_op | source)
XLA Modules:
  0.0 441.7 jit_solution(5581959899953794531)
XLA Ops:
  11.1 7.4 %all_to_all.14 = bf16[4,128,128]{2,1,0:T(8,128)(2,1)S(1)} all-to-all(bf16[4,128,128]{2,1,0:T(8,128)(2,1)S(1)} %bitcast.130), channel_id=1, replica_groups=mesh['row'=2,'col'=2,'rhs'=64] {'row','col'}, dimensions={0} | all-to-all | bytes 262144 | tf_op jit(solution)/shard_map/all_to_all | solution.py:79
  18.5 5.2 %stack.36 = bf16[64,32,2048]{2,1,0:T(8,128)(2,1)} broadcast(bf16[32,2048]{1,0:T(8,128)(2,1)} %param.11), dimensions={1,2} | broadcast | bytes 8519680 | tf_op jit(solution)/shard_map/stack | solution.py:85
  23.7 12.6 %all-to-all-start.1 = ((bf16[64,32,2048]{2,1,0:T(8,128)(2,1)}), bf16[64,32,2048]{2,1,0:T(8,128)(2,1)}, u32[]{:S(2)}, u32[]{:S(2)}) async-start(bf16[64,32,2048]{2,1,0:T(8,128)(2,1)} %stack.36), calls=%async_computation.1 | async-start | bytes 16777216 | tf_op jit(solution)/shard_map/all_to_all | solution.py:84
  37.8 168.4 %all-gather.2.cloned.1.call-done = bf16[512,2048]{1,0:T(8,128)(2,1)} async-done(((bf16[8,2048]{1,0:T(8,128)(2,1)}), bf16[512,2048]{1,0:T(8,128)(2,1)}) %all-gather.2.cloned.1.call-update) | async-done | bytes 2097168 | tf_op jit(solution)/shard_map/all_gather | solution.py:82
  206.1 2.1 fusion.80
  208.3 1.5 collective-permute-start
  212.2 1.5 copy.12
  213.8 18.6 %all-to-all-done.1 = bf16[64,32,2048]{2,1,0:T(8,128)(2,1)} async-done(((bf16[64,32,2048]{2,1,0:T(8,128)(2,1)}), bf16[64,32,2048]{2,1,0:T(8,128)(2,1)}, u32[]{:S(2)}, u32[]{:S(2)}) %all-to-all-start.1) | async-done | bytes 8388640 | tf_op jit(solution)/shard_map/all_to_all | solution.py:84
  245.0 1.5 fusion.45
  258.7 2.2 fusion.85
  261.0 64.9 %while.34 = (s32[]{:T(128)}, f32[2048,128]{1,0:T(8,128)S(1)}, bf16[2048,128]{1,0:T(8,128)(2,1)S(1)}, bf16[2048,2048]{1,0:T(8,128)(2,1)}, f32[16,128,128]{2,1,0:T...) while((s32[]{:T(128)}, f32[2048,128]{1,0:T(8,128)S(1)}, ...), condition=%wide.region_3.4_spmd, body=%wide.region_2.3_spmd.sunk | while | flops 160006144 | bytes 5639389 | solution.py:55
  263.6 1.5 fusion.124
  267.6 1.5 fusion.124
  271.7 1.5 fusion.124
  275.7 1.5 fusion.124
  279.8 1.5 fusion.124
  283.8 1.5 fusion.124
  287.9 1.5 fusion.124
  292.0 1.5 fusion.124
  296.0 1.5 fusion.124
  300.1 1.5 fusion.124
  304.1 1.5 fusion.124
  312.2 1.5 fusion.124
  320.3 1.5 fusion.124
  325.9 4.0 collective-permute-start.1
  329.8 8.4 %collective-permute-done.1 = bf16[2048,128]{1,0:T(8,128)(2,1)S(1)} collective-permute-done((bf16[2048,128]{1,0:T(8,128)(2,1)S(1)}, bf16[2048,128]{1,0:T(8,128)(2,1)S(1)}, u32[]{:S(2)}, u32[]{:S(2)}) %collective-permute-start.1) | collective-permute-done | bytes 524320 | tf_op jit(solution)/shard_map/ppermute | solution.py:105
  338.3 4.7 %fusion.48 = f32[128,2048]{1,0:T(8,128)S(1)} fusion(bf16[2048,2048]{1,0:T(8,128)(2,1)} %bitcast.12, bf16[2048,128]{1,0:T(8,128)(2,1)S(1)} %broadcast_select_fusion), kind=kOutput, calls=%fused_computation.67 | convolution fusion | flops 1074528256 | bytes 9961472 | tf_op jit(solution)/shard_map/dot_general | solution.py:15
  343.0 4.7 %fusion.29 = bf16[2048,128]{0,1:T(8,128)(2,1)S(1)} fusion(f32[128,2048]{1,0:T(8,128)S(1)} %fusion.80, f32[128,2048]{1,0:T(8,128)S(1)} %fusion.48, bf16[2048,128]{1,0:T(8,128)(2,1)S(1)} %broadcast_select_fusion, bf16[2048,2048]{1,0:T(8,128)(2,1)} %bitcast.12, pred[]{:T(512)S(6)} %eq.49), kind=kOutput, calls=%fused_computation.44 | convolution fusion | flops 1075052544 | bytes 11534337 | tf_op jit(solution)/shard_map/dot_general | solution.py:14
  349.0 2.5 collective-permute-done.2
  353.2 64.8 %while.35 = (s32[]{:T(128)}, f32[2048,128]{1,0:T(8,128)S(1)}, bf16[2048,128]{1,0:T(8,128)(2,1)S(1)}, bf16[2048,2048]{1,0:T(8,128)(2,1)}, f32[16,128,128]{2,1,0:T...) while((s32[]{:T(128)}, f32[2048,128]{1,0:T(8,128)S(1)}, ...), condition=%wide.region_5.6_spmd, body=%wide.region_4.5_spmd.sunk | while | flops 160006144 | bytes 5639389 | solution.py:55
  355.7 1.5 fusion.130
  419.3 14.7 %collective-permute-done.3 = bf16[2048,128]{1,0:T(8,128)(2,1)S(1)} collective-permute-done((bf16[2048,128]{1,0:T(8,128)(2,1)S(1)}, bf16[2048,128]{1,0:T(8,128)(2,1)S(1)}, u32[]{:S(2)}, u32[]{:S(2)}) %collective-permute-start.3) | collective-permute-done | bytes 524320 | tf_op jit(solution)/shard_map/ppermute | solution.py:114
  (182 shorter events, 145.8 us)
Async XLA Ops:
  6.5 3.6 copy-start
  23.7 13.4 %copy-start.3 = (s32[8]{0:T(128)S(1)}, s32[8]{0:T(128)}, u32[]{:S(2)}) copy-start(s32[8]{0:T(128)} %param.14) | copy-start | bytes 100
  23.7 186.1 %copy-start.2 = (bf16[2048,128]{1,0:T(8,128)(2,1)S(1)}, bf16[2048,128]{1,0:T(8,128)(2,1)}, u32[]{:S(2)}) copy-start(bf16[2048,128]{1,0:T(8,128)(2,1)} %param.17) | copy-start | bytes 1572868
  23.7 208.7 %all-to-all-start.1 = ((bf16[64,32,2048]{2,1,0:T(8,128)(2,1)}), bf16[64,32,2048]{2,1,0:T(8,128)(2,1)}, u32[]{:S(2)}, u32[]{:S(2)}) async-start(bf16[64,32,2048]{2,1,0:T(8,128)(2,1)} %stack.36), calls=%async_computation.1 | async-start | bytes 16777216 | tf_op jit(solution)/shard_map/all_to_all | solution.py:84
  36.4 169.8 %all-gather.2.cloned.1.call-start = ((), (), s32[]{:S(2)}) async-start(), calls=%async_computation.2 | async-start | bytes 2129920 | tf_op jit(solution)/shard_map/all_gather | solution.py:82
  208.3 2.8 collective-permute-start
  325.9 12.4 %collective-permute-start.1 = (bf16[2048,128]{1,0:T(8,128)(2,1)S(1)}, bf16[2048,128]{1,0:T(8,128)(2,1)S(1)}, u32[]{:S(2)}, u32[]{:S(2)}) collective-permute-start(bf16[2048,128]{1,0:T(8,128)(2,1)S(1)} %get-tuple-element.313), channel_id=1, source_target_pairs={{64,0},{65,1},{66,2},{67,3},{68,4},{69,5},{70,6},{71,7},{72,8},{73... | collective-permute-start | bytes 1572872 | tf_op jit(solution)/shard_map/ppermute | solution.py:105
  347.7 1.3 copy-start.1
  347.7 3.8 collective-permute-start.2
  418.0 16.0 %collective-permute-start.3 = (bf16[2048,128]{1,0:T(8,128)(2,1)S(1)}, bf16[2048,128]{1,0:T(8,128)(2,1)S(1)}, u32[]{:S(2)}, u32[]{:S(2)}) collective-permute-start(bf16[2048,128]{1,0:T(8,128)(2,1)S(1)} %get-tuple-element.314), channel_id=1, source_target_pairs={{0,64},{1,65},{2,66},{3,67},{4,68},{5,69},{6,70},{7,71},{8,72},{9,... | collective-permute-start | bytes 1572872 | tf_op jit(solution)/shard_map/ppermute | solution.py:114
Sparse Core Ops, SparseCore 0:
  40.7 165.3 all-gather.1
